TPU v7x, 128 devices: a whole 4x4x4 slice. The times are simulated.
128 devices in a mesh: tok: 16 (over x, y), voc: 8 (over z, core).
Axes of the slice: x: 4, y: 4, z: 4, core: 2. Of those that a mesh axis runs over, the one named last changes fastest.
Arguments:
- hidden_rows: bfloat16 [512, 3584], P(('tok', 'voc')), may hold values from -40 to 40
- head_weight: bfloat16 [147456, 3584], P(('tok', 'voc')), may hold values from -0.09375 to 0.09375
- teacher_index: int32 [512, 64], replicated, may hold values from 0 to 147455, as said below
- teacher_logprob: float32 [512, 64], replicated, may hold values from -10 to -4.2
Outputs:
- row_loss: float32 [512], P(('tok', 'voc'))
- head_grad: bfloat16 [147456, 3584], P(('tok', 'voc'))
- input_grad: bfloat16 [512, 3584], P(('tok', 'voc'))
Inputs may be any that keep to these rules, and one draw needn't show every extreme that they name: `teacher_index`: the 64 entries of one token are distinct.
All inputs are finite; a program needn't handle non-finite values.
Results may differ from a plain program's by a relative error of at most 0.015.
Values may be sent and summed in bfloat16 or wider, within the bound.
No kernel may reach another device: no remote copies, remote signals or barrier semaphores. Data moves between devices by JAX's collectives and lax.ppermute only.
A program may use at most 128 MiB of HBM per device.

v0:
```python
import jax
import jax.numpy as jnp
from jax import lax
from jax.sharding import PartitionSpec as P

loss_scale = 256.0


def teacher_target(local, probs, voc_dev):
    blocks = local.shape[0] // 64
    local_b = local.reshape(blocks, 64, local.shape[1])
    probs_b = probs.reshape(blocks, 64, probs.shape[1])
    columns = jnp.arange(voc_dev, dtype=jnp.int32)[None, None, :]

    def one_block(args):
        block_local, block_probs = args
        equal = block_local[:, :, None] == columns
        return jnp.sum(jnp.where(equal, block_probs[:, :, None], 0.0), axis=1)

    return lax.map(one_block, (local_b, probs_b)).reshape(local.shape[0], voc_dev)


def per_device(hidden_rows, head_weight, teacher_index, teacher_logprob):
    voc_dev = head_weight.shape[0]
    tok_dev = hidden_rows.shape[0]
    every = lax.all_gather(hidden_rows, ("tok", "voc"), axis=0, tiled=True)
    logits = lax.dot_general(
        every, head_weight, (((1,), (1,)), ((), ())), preferred_element_type=jnp.float32
    )
    position = lax.axis_index(("tok", "voc"))
    offset = position * voc_dev
    local = teacher_index - offset
    probs = jnp.exp(teacher_logprob)
    target = teacher_target(local, probs, voc_dev)
    part_dot = jnp.sum(logits * target, axis=1)
    local_peak = jnp.max(logits, axis=1)
    peak = lax.pmax(local_peak, ("tok", "voc"))
    summed, dotted = lax.psum(
        (jnp.sum(jnp.exp(logits - peak[:, None]), axis=1), part_dot), ("tok", "voc")
    )
    lse = peak + jnp.log(summed)
    total_p = jnp.sum(probs, axis=1)
    own_term = jnp.sum(probs * teacher_logprob, axis=1)
    loss_all = own_term - dotted + total_p * lse
    row_loss = lax.dynamic_slice_in_dim(loss_all, position * tok_dev, tok_dev, 0)
    grad = (loss_scale * (total_p[:, None] * jnp.exp(logits - lse[:, None]) - target)).astype(
        jnp.bfloat16
    )
    head_grad = lax.dot_general(
        grad, every, (((0,), (0,)), ((), ())), preferred_element_type=jnp.float32
    ).astype(jnp.bfloat16)
    input_sum = lax.psum_scatter(
        jnp.dot(grad, head_weight, preferred_element_type=jnp.float32),
        ("tok", "voc"),
        scatter_dimension=0,
        tiled=True,
    )
    return (row_loss, head_grad, input_sum.astype(jnp.bfloat16))


def solution(mesh):
    placed = (P(("tok", "voc"), None), P(("tok", "voc"), None), P(), P())
    return jax.shard_map(
        per_device,
        mesh=mesh,
        in_specs=placed,
        out_specs=(P(("tok", "voc")), P(("tok", "voc"), None), P(("tok", "voc"), None)),
        check_vma=False,
    )
```

profile of v0, /device:TPU:0, one launch (start us, length us, event | category | flops | bytes accessed | tf_op | source)
XLA Modules:
  0.0 364.6 jit_solution(16396800213007242610)
XLA Ops:
  7.2 0.7 all-gather.3.cloned.1.call-update
  7.9 0.9 broadcast_subtract_fusion
  9.0 1.0 multiply_reduce_fusion
  10.1 28.0 %while.11 = (s32[]{:T(128)}, f32[8,64,1152]{2,1,0:T(8,128)S(1)}, s32[8,64,64]{2,1,0:T(8,128)S(1)}, f32[8,64,64]{2,1,0:T(8,128)S(1)}, s32[]{:T(128)}) while((s32[]{:T(128)}, f32[8,64,1152]{2,1,0:T(8,128)S(1)}, s32[8,64,64]{2,1,0:T(8,128)S(1)}, f32[8,64,64]{2,1,0:T(8,128)S(1)}, s32[]{:T(128)}) %tuple.35), condition=%wide.region_3.4_spmd.clone, body=%wide.region_1.3_spmd.clone.sunk | while | flops 14082050 | bytes 983113 | solution.py:20
  10.1 3.4 select_reduce_fusion.2
  13.6 3.4 select_reduce_fusion.2
  17.1 3.4 select_reduce_fusion.2
  20.6 3.4 select_reduce_fusion.2
  24.1 3.4 select_reduce_fusion.2
  27.6 3.4 select_reduce_fusion.2
  31.1 3.4 select_reduce_fusion.2
  34.6 3.4 select_reduce_fusion.2
  38.1 41.7 %all-gather.3.cloned.1.call-done = bf16[128,4,3584]{2,1,0:T(4,128)(2,1)} async-done(((bf16[1,4,3584]{2,1,0:T(4,128)(2,1)}), bf16[128,4,3584]{2,1,0:T(4,128)(2,1)}) %all-gather.3.cloned.1.call-update) | async-done | bytes 3670032 | tf_op jit(solution)/shard_map/all_gather | solution.py:26
  79.8 6.7 %reshape.26 = bf16[512,3584]{1,0:T(8,128)(2,1)} reshape(bf16[128,4,3584]{2,1,0:T(4,128)(2,1)} %all-gather.3.cloned.1.call-done) | data formatting | bytes 7340032
  86.5 10.9 %fusion.5 = (f32[512]{0:T(512)S(1)}, f32[512,1152]{1,0:T(8,128)}) fusion(bf16[512,3584]{1,0:T(8,128)(2,1)} %reshape.26, bf16[1152,3584]{1,0:T(8,128)(2,1)} %param.7), kind=kOutput, calls=%fused_computation.19 | convolution fusion | flops 4228447744 | bytes 14288896 | tf_op jit(solution)/shard_map/dot_general | solution.py:27
  97.4 62.7 %pmax.7 = f32[512]{0:T(512)S(1)} all-reduce(f32[512]{0:T(512)S(1)} %get-tuple-element.56), channel_id=1, replica_groups=mesh['tok'=16,'voc'=8] {'tok','voc'}, use_global_device_ids=true, to_apply=%region_8.9 | all-reduce | flops 512 | bytes 4096 | tf_op jit(solution)/shard_map/pmax | solution.py:37
  160.1 2.3 fusion.2
  162.4 64.3 %psum.15 = f32[512]{0:T(512)S(1)} all-reduce(f32[512]{0:T(512)S(1)} %get-tuple-element.42), channel_id=1, replica_groups=mesh['tok'=16,'voc'=8] {'tok','voc'}, use_global_device_ids=true, to_apply=%region_10.11 | all-reduce | flops 512 | bytes 4096 | tf_op jit(solution)/shard_map/psum | solution.py:38
  226.7 2.6 fusion.4
  229.3 10.4 %fusion.6 = f32[512,3584]{1,0:T(8,128)} fusion(bf16[512,1152]{1,0:T(8,128)(2,1)S(1)} %fusion.4, bf16[1152,3584]{1,0:T(8,128)(2,1)} %param.7), kind=kOutput, calls=%fused_computation.20 | convolution fusion | flops 4227858432 | bytes 16777216 | tf_op jit(solution)/shard_map/dot_general | solution.py:53
  239.7 6.7 %convolution_convert_fusion = bf16[1152,3584]{1,0:T(8,128)(2,1)} fusion(bf16[512,1152]{1,0:T(8,128)(2,1)S(1)} %fusion.4, bf16[512,3584]{1,0:T(8,128)(2,1)S(1)} %copy-done), kind=kOutput, calls=%fused_computation.6 | convolution fusion | flops 4231987200 | bytes 13107200 | tf_op jit(solution)/shard_map/dot_general | solution.py:49
  246.4 109.3 %all-reduce.3 = (f32[512]{0:T(512)S(1)}, bf16[512,3584]{1,0:T(8,128)(2,1)}) all-reduce(f32[512]{0:T(512)S(1)} %get-tuple-element.41, f32[512,3584]{1,0:T(8,128)} %fusion.6), channel_id=1, replica_groups=mesh['tok'=16,'voc'=8] {'tok','voc'}, use_global_device_ids=true, to_apply=%region_5.6 | all-reduce | flops 1835520 | bytes 11014144 | tf_op jit(solution)/shard_map/psum | solution.py:38
  355.7 0.6 dynamic_slice.11
  356.3 1.4 dynamic-slice_convert_fusion
  (32 shorter events, 0.7 us)
Async XLA Ops:
  7.2 72.6 %all-gather.3.cloned.1.call-start = ((), (), s32[]{:S(2)}) async-start(), calls=%async_computation | async-start | bytes 3698688 | tf_op jit(solution)/shard_map/all_gather | solution.py:26
  229.3 10.4 %copy-start = (bf16[512,3584]{1,0:T(8,128)(2,1)S(1)}, bf16[512,3584]{1,0:T(8,128)(2,1)}, u32[]{:S(2)}) copy-start(bf16[512,3584]{1,0:T(8,128)(2,1)} %reshape.26) | copy-start | bytes 11010052
Sparse Core Ops, SparseCore 0:
  11.0 68.7 all-gather.2
where the time goes:
time: 365 us
  blocking collectives  236 us (65%)
  waiting for transfers between devices  42.4 us (12%)
  other arithmetic  34 us (9%)
  matrix products  28 us (8%)
  between operations  14.1 us (4%)
  local copies, waits for them, and re-layouts  9.39 us (3%)
    psum x2, blocking collectives, per_device(): lax.psum((jnp.sum(jnp.exp(logits - peak[:, None]), axis=1), part_dot), ('...  174 us
    pmax x1, blocking collectives, per_device(): peak = lax.pmax(local_peak, ('tok', 'voc'))  62.7 us
    all_gather x1, waiting for transfers between devices, per_device(): every = lax.all_gather(hidden_rows, ('tok', 'voc'), axis=0, tiled=True)  41.7 us
    reduce_sum x8, other arithmetic, one_block(): return jnp.sum(jnp.where(equal, block_probs[:, :, None], 0.0), axis=1)  27.2 us
    dot_general x1, matrix products, per_device(): lax.dot_general(every, head_weight, (((1,), (1,)), ((), ())), preferred_e...  10.9 us
    dot_general x1, matrix products, per_device(): jnp.dot(grad, head_weight, preferred_element_type=jnp.float32)  10.4 us
  transfers between devices with their start and end apart: 1, of which 1 were waited for; matrix products, arithmetic and copies ran while one was open for 8% of the time, Pallas kernels for 0%

commit v1 on v0

--- a/solution.py
+++ b/solution.py
@@ -4,6 +4,11 @@
 from jax.sharding import PartitionSpec as P
 
 loss_scale = 256.0
+
+
+def one_after_other(value, one, other):
+    inner = lax.psum(value, one)
+    return lax.psum(inner, other)
 
 
 def teacher_target(local, probs, voc_dev):
@@ -35,8 +40,8 @@
     part_dot = jnp.sum(logits * target, axis=1)
     local_peak = jnp.max(logits, axis=1)
     peak = lax.pmax(local_peak, ("tok", "voc"))
-    summed, dotted = lax.psum(
-        (jnp.sum(jnp.exp(logits - peak[:, None]), axis=1), part_dot), ("tok", "voc")
+    summed, dotted = one_after_other(
+        (jnp.sum(jnp.exp(logits - peak[:, None]), axis=1), part_dot), "tok", "voc"
     )
     lse = peak + jnp.log(summed)
     total_p = jnp.sum(probs, axis=1)

time: 365 us -> 351 us (0.962)
  blocking collectives: 236 us -> 223 us
    psum x2, blocking collectives: 174 us -> 50.5 us  [the longest x1 38.1 us: one_after_other(): inner = lax.psum(value, one)]
    unnamed x0 -> x1, blocking collectives: none -> 109 us
where the time goes in v1:
time: 351 us
  blocking collectives  223 us (64%)
  waiting for transfers between devices  42.4 us (12%)
  other arithmetic  34 us (10%)
  matrix products  28 us (8%)
  between operations  14.1 us (4%)
  local copies, waits for them, and re-layouts  9.38 us (3%)
    unnamed x1, blocking collectives  109 us
    pmax x1, blocking collectives, per_device(): peak = lax.pmax(local_peak, ('tok', 'voc'))  62.7 us
    all_gather x1, waiting for transfers between devices, per_device(): every = lax.all_gather(hidden_rows, ('tok', 'voc'), axis=0, tiled=True)  41.7 us
    psum x1, blocking collectives, one_after_other(): inner = lax.psum(value, one)  38.1 us
    reduce_sum x8, other arithmetic, one_block(): return jnp.sum(jnp.where(equal, block_probs[:, :, None], 0.0), axis=1)  27.2 us
    psum x1, blocking collectives, one_after_other(): return lax.psum(inner, other)  12.4 us
    dot_general x1, matrix products, per_device(): lax.dot_general(every, head_weight, (((1,), (1,)), ((), ())), preferred_e...  10.9 us
    dot_general x1, matrix products, per_device(): jnp.dot(grad, head_weight, preferred_element_type=jnp.float32)  10.4 us
  transfers between devices with their start and end apart: 1, of which 1 were waited for; matrix products, arithmetic and copies ran while one was open for 8% of the time, Pallas kernels for 0%

profile of v1, /device:TPU:0, one launch (start us, length us, event | category | flops | bytes accessed | tf_op | source)
XLA Modules:
  0.0 350.9 jit_solution(14541141673544069546)
XLA Ops:
  7.2 0.7 all-gather.3.cloned.1.call-update
  7.9 0.9 broadcast_subtract_fusion
  9.0 1.0 multiply_reduce_fusion
  10.1 28.0 %while.11 = (s32[]{:T(128)}, f32[8,64,1152]{2,1,0:T(8,128)S(1)}, s32[8,64,64]{2,1,0:T(8,128)S(1)}, f32[8,64,64]{2,1,0:T(8,128)S(1)}, s32[]{:T(128)}) while((s32[]{:T(128)}, f32[8,64,1152]{2,1,0:T(8,128)S(1)}, s32[8,64,64]{2,1,0:T(8,128)S(1)}, f32[8,64,64]{2,1,0:T(8,128)S(1)}, s32[]{:T(128)}) %tuple.36), condition=%wide.region_3.4_spmd.clone, body=%wide.region_1.3_spmd.clone.sunk | while | flops 14082050 | bytes 983113 | solution.py:25
  10.1 3.4 select_reduce_fusion.2
  13.6 3.4 select_reduce_fusion.2
  17.1 3.4 select_reduce_fusion.2
  20.6 3.4 select_reduce_fusion.2
  24.1 3.4 select_reduce_fusion.2
  27.6 3.4 select_reduce_fusion.2
  31.1 3.4 select_reduce_fusion.2
  34.6 3.4 select_reduce_fusion.2
  38.1 41.7 %all-gather.3.cloned.1.call-done = bf16[128,4,3584]{2,1,0:T(4,128)(2,1)} async-done(((bf16[1,4,3584]{2,1,0:T(4,128)(2,1)}), bf16[128,4,3584]{2,1,0:T(4,128)(2,1)}) %all-gather.3.cloned.1.call-update) | async-done | bytes 3670032 | tf_op jit(solution)/shard_map/all_gather | solution.py:31
  79.8 6.7 %reshape.26 = bf16[512,3584]{1,0:T(8,128)(2,1)} reshape(bf16[128,4,3584]{2,1,0:T(4,128)(2,1)} %all-gather.3.cloned.1.call-done) | data formatting | bytes 7340032
  86.5 10.9 %fusion.5 = (f32[512]{0:T(512)S(1)}, f32[512,1152]{1,0:T(8,128)}) fusion(bf16[512,3584]{1,0:T(8,128)(2,1)} %reshape.26, bf16[1152,3584]{1,0:T(8,128)(2,1)} %param.7), kind=kOutput, calls=%fused_computation.19 | convolution fusion | flops 4228447744 | bytes 14288896 | tf_op jit(solution)/shard_map/dot_general | solution.py:32
  97.4 62.7 %pmax.7 = f32[512]{0:T(512)S(1)} all-reduce(f32[512]{0:T(512)S(1)} %get-tuple-element.60), channel_id=1, replica_groups=mesh['tok'=16,'voc'=8] {'tok','voc'}, use_global_device_ids=true, to_apply=%region_9.10 | all-reduce | flops 512 | bytes 4096 | tf_op jit(solution)/shard_map/pmax | solution.py:42
  160.1 2.3 fusion.2
  162.4 38.1 %all-reduce.1 = (f32[512]{0:T(512)S(1)}, f32[512]{0:T(512)S(1)}) all-reduce(f32[512]{0:T(512)S(1)} %get-tuple-element.42, f32[512]{0:T(512)S(1)} %get-tuple-element.41), channel_id=1, replica_groups=mesh['tok'=16,'voc'=8] {'tok'}, use_global_device_ids=true, to_apply=%region_11.12 | all-reduce | flops 1024 | bytes 8192 | tf_op jit(solution)/shard_map/psum | solution.py:10
  200.6 12.4 %all-reduce.2 = (f32[512]{0:T(512)S(1)}, f32[512]{0:T(512)S(1)}) all-reduce(f32[512]{0:T(512)S(1)} %get-tuple-element.53, f32[512]{0:T(512)S(1)} %get-tuple-element.54), channel_id=1, replica_groups=mesh['tok'=16,'voc'=8] {'voc'}, use_global_device_ids=true, to_apply=%region_12.13 | all-reduce | flops 1024 | bytes 8192 | tf_op jit(solution)/shard_map/psum | solution.py:11
  213.0 2.6 fusion.4
  215.6 10.4 %fusion.6 = f32[512,3584]{1,0:T(8,128)} fusion(bf16[512,1152]{1,0:T(8,128)(2,1)S(1)} %fusion.4, bf16[1152,3584]{1,0:T(8,128)(2,1)} %param.7), kind=kOutput, calls=%fused_computation.20 | convolution fusion | flops 4227858432 | bytes 16777216 | tf_op jit(solution)/shard_map/dot_general | solution.py:58
  226.0 6.7 %convolution_convert_fusion = bf16[1152,3584]{1,0:T(8,128)(2,1)} fusion(bf16[512,1152]{1,0:T(8,128)(2,1)S(1)} %fusion.4, bf16[512,3584]{1,0:T(8,128)(2,1)S(1)} %copy-done), kind=kOutput, calls=%fused_computation.6 | convolution fusion | flops 4231987200 | bytes 13107200 | tf_op jit(solution)/shard_map/dot_general | solution.py:54
  232.7 109.3 %all-reduce.4 = bf16[512,3584]{1,0:T(8,128)(2,1)} all-reduce(f32[512,3584]{1,0:T(8,128)} %fusion.6), channel_id=2, replica_groups=mesh['tok'=16,'voc'=8] {'tok','voc'}, use_global_device_ids=true, to_apply=%region_13.14.clone | all-reduce | flops 1835008 | bytes 11010048
  342.0 1.4 dynamic-slice_convert_fusion
  (32 shorter events, 1.3 us)
Async XLA Ops:
  7.2 72.6 %all-gather.3.cloned.1.call-start = ((), (), s32[]{:S(2)}) async-start(), calls=%async_computation | async-start | bytes 3698688 | tf_op jit(solution)/shard_map/all_gather | solution.py:31
  215.6 10.4 %copy-start = (bf16[512,3584]{1,0:T(8,128)(2,1)S(1)}, bf16[512,3584]{1,0:T(8,128)(2,1)}, u32[]{:S(2)}) copy-start(bf16[512,3584]{1,0:T(8,128)(2,1)} %reshape.26) | copy-start | bytes 11010052
Sparse Core Ops, SparseCore 0:
  11.0 68.7 all-gather.2

commit v2 on v0

--- a/solution.py
+++ b/solution.py
@@ -23,7 +23,12 @@
 def per_device(hidden_rows, head_weight, teacher_index, teacher_logprob):
     voc_dev = head_weight.shape[0]
     tok_dev = hidden_rows.shape[0]
-    every = lax.all_gather(hidden_rows, ("tok", "voc"), axis=0, tiled=True)
+    every = jnp.concatenate(
+        lax.all_to_all(
+            jnp.stack([hidden_rows] * lax.axis_size(("tok", "voc")), axis=0), ("tok", "voc"), 0, 0
+        ),
+        axis=0,
+    )
     logits = lax.dot_general(
         every, head_weight, (((1,), (1,)), ((), ())), preferred_element_type=jnp.float32
     )

time: 365 us -> 341 us (0.934)
  waiting for transfers between devices: 42.4 us -> 18.8 us
  between operations: 14.1 us -> 0.73 us
  starting transfers between devices: 0.04 us -> 11.6 us
    all_gather x1 -> x0, waiting for transfers between devices: 41.7 us -> none  [per_device(): every = lax.all_gather(hidden_rows, ('tok', 'voc'), axis=0, tiled=True)]
    all_to_all x0 -> x1, waiting for transfers between devices: none -> 18.8 us  [per_device(): lax.all_to_all(jnp.stack([hidden_rows] * lax.axis_size(('tok', 'voc')), a...]
    all_to_all x0 -> x1, starting transfers between devices: none -> 11.6 us  [per_device(): lax.all_to_all(jnp.stack([hidden_rows] * lax.axis_size(('tok', 'voc')), a...]
    reshape x0 -> x1, local copies, waits for them, and re-layouts: none -> 6.73 us  [per_device(): jnp.concatenate(lax.all_to_all(jnp.stack([hidden_rows] * lax.axis_size(('...]
    unnamed x3 -> x6, local copies, waits for them, and re-layouts: 6.74 us -> 0.01 us
where the time goes in v2:
time: 341 us; the launch traced here: 340 us
  blocking collectives  235 us (69%)
  other arithmetic  32.2 us (9%)
  matrix products  28 us (8%)
  waiting for transfers between devices  18.8 us (6%)
  local copies, waits for them, and re-layouts  12.9 us (4%)
  starting transfers between devices  11.6 us (3%)
    psum x2, blocking collectives, per_device(): lax.psum((jnp.sum(jnp.exp(logits - peak[:, None]), axis=1), part_dot), ('...  173 us
    pmax x1, blocking collectives, per_device(): peak = lax.pmax(local_peak, ('tok', 'voc'))  62.5 us
    reduce_sum x8, other arithmetic, one_block(): return jnp.sum(jnp.where(equal, block_probs[:, :, None], 0.0), axis=1)  27.2 us
    all_to_all x1, waiting for transfers between devices, per_device(): lax.all_to_all(jnp.stack([hidden_rows] * lax.axis_size(('tok', 'voc')), a...  18.8 us
    all_to_all x1, starting transfers between devices, per_device(): lax.all_to_all(jnp.stack([hidden_rows] * lax.axis_size(('tok', 'voc')), a...  11.6 us
    dot_general x1, matrix products, per_device(): lax.dot_general(every, head_weight, (((1,), (1,)), ((), ())), preferred_e...  10.9 us
    dot_general x1, matrix products, per_device(): jnp.dot(grad, head_weight, preferred_element_type=jnp.float32)  10.4 us
  transfers between devices with their start and end apart: 1, of which 1 were waited for; matrix products, arithmetic and copies ran while one was open for 8% of the time, Pallas kernels for 0%

profile of v2, /device:TPU:0, one launch (start us, length us, event | category | flops | bytes accessed | tf_op | source)
XLA Modules:
  0.0 339.9 jit_solution(12822126608999091527)
XLA Ops:
  0.6 3.5 %stack.2 = bf16[128,4,3584]{2,1,0:T(4,128)(2,1)} broadcast(bf16[4,3584]{1,0:T(4,128)(2,1)} %param.6), dimensions={1,2} | broadcast | bytes 3698688 | tf_op jit(solution)/shard_map/stack | solution.py:28
  4.2 11.6 %all-to-all-start = ((bf16[128,4,3584]{2,1,0:T(4,128)(2,1)}), bf16[128,4,3584]{2,1,0:T(4,128)(2,1)}, u32[]{:S(2)}, u32[]{:S(2)}) async-start(bf16[128,4,3584]{2,1,0:T(4,128)(2,1)} %stack.2), calls=%async_computation | async-start | bytes 7340032 | tf_op jit(solution)/shard_map/all_to_all | solution.py:27
  15.8 0.1 copy.11
  16.1 28.0 %while.11 = (s32[]{:T(128)}, f32[8,64,1152]{2,1,0:T(8,128)S(1)}, s32[8,64,64]{2,1,0:T(8,128)S(1)}, f32[8,64,64]{2,1,0:T(8,128)S(1)}, s32[]{:T(128)}) while((s32[]{:T(128)}, f32[8,64,1152]{2,1,0:T(8,128)S(1)}, s32[8,64,64]{2,1,0:T(8,128)S(1)}, f32[8,64,64]{2,1,0:T(8,128)S(1)}, s32[]{:T(128)}) %tuple.33), condition=%wide.region_3.4_spmd.clone, body=%wide.region_1.3_spmd.clone.sunk | while | flops 14082050 | bytes 983113 | solution.py:20
  16.2 3.4 %select_reduce_fusion.2 = f32[64,1152]{1,0:T(8,128)S(1)} fusion(f32[64,64]{1,0:T(8,128)S(1)} %dynamic-slice_bitcast_fusion.4, s32[64,64]{1,0:T(8,128)S(1)} %dynamic-slice_bitcast_fusion.5), kind=kLoop, calls=%fused_computation.2.clone.1 | loop fusion | flops 14082048 | bytes 327680 | tf_op jit(solution)/shard_map/while/body/eval_jaxpr/reduce_sum | solution.py:18
  19.7 3.4 %select_reduce_fusion.2 = f32[64,1152]{1,0:T(8,128)S(1)} fusion(f32[64,64]{1,0:T(8,128)S(1)} %dynamic-slice_bitcast_fusion.4, s32[64,64]{1,0:T(8,128)S(1)} %dynamic-slice_bitcast_fusion.5), kind=kLoop, calls=%fused_computation.2.clone.1 | loop fusion | flops 14082048 | bytes 327680 | tf_op jit(solution)/shard_map/while/body/eval_jaxpr/reduce_sum | solution.py:18
  23.2 3.4 %select_reduce_fusion.2 = f32[64,1152]{1,0:T(8,128)S(1)} fusion(f32[64,64]{1,0:T(8,128)S(1)} %dynamic-slice_bitcast_fusion.4, s32[64,64]{1,0:T(8,128)S(1)} %dynamic-slice_bitcast_fusion.5), kind=kLoop, calls=%fused_computation.2.clone.1 | loop fusion | flops 14082048 | bytes 327680 | tf_op jit(solution)/shard_map/while/body/eval_jaxpr/reduce_sum | solution.py:18
  26.7 3.4 %select_reduce_fusion.2 = f32[64,1152]{1,0:T(8,128)S(1)} fusion(f32[64,64]{1,0:T(8,128)S(1)} %dynamic-slice_bitcast_fusion.4, s32[64,64]{1,0:T(8,128)S(1)} %dynamic-slice_bitcast_fusion.5), kind=kLoop, calls=%fused_computation.2.clone.1 | loop fusion | flops 14082048 | bytes 327680 | tf_op jit(solution)/shard_map/while/body/eval_jaxpr/reduce_sum | solution.py:18
  30.2 3.4 %select_reduce_fusion.2 = f32[64,1152]{1,0:T(8,128)S(1)} fusion(f32[64,64]{1,0:T(8,128)S(1)} %dynamic-slice_bitcast_fusion.4, s32[64,64]{1,0:T(8,128)S(1)} %dynamic-slice_bitcast_fusion.5), kind=kLoop, calls=%fused_computation.2.clone.1 | loop fusion | flops 14082048 | bytes 327680 | tf_op jit(solution)/shard_map/while/body/eval_jaxpr/reduce_sum | solution.py:18
  33.7 3.4 %select_reduce_fusion.2 = f32[64,1152]{1,0:T(8,128)S(1)} fusion(f32[64,64]{1,0:T(8,128)S(1)} %dynamic-slice_bitcast_fusion.4, s32[64,64]{1,0:T(8,128)S(1)} %dynamic-slice_bitcast_fusion.5), kind=kLoop, calls=%fused_computation.2.clone.1 | loop fusion | flops 14082048 | bytes 327680 | tf_op jit(solution)/shard_map/while/body/eval_jaxpr/reduce_sum | solution.py:18
  37.2 3.4 %select_reduce_fusion.2 = f32[64,1152]{1,0:T(8,128)S(1)} fusion(f32[64,64]{1,0:T(8,128)S(1)} %dynamic-slice_bitcast_fusion.4, s32[64,64]{1,0:T(8,128)S(1)} %dynamic-slice_bitcast_fusion.5), kind=kLoop, calls=%fused_computation.2.clone.1 | loop fusion | flops 14082048 | bytes 327680 | tf_op jit(solution)/shard_map/while/body/eval_jaxpr/reduce_sum | solution.py:18
  40.7 3.4 %select_reduce_fusion.2 = f32[64,1152]{1,0:T(8,128)S(1)} fusion(f32[64,64]{1,0:T(8,128)S(1)} %dynamic-slice_bitcast_fusion.4, s32[64,64]{1,0:T(8,128)S(1)} %dynamic-slice_bitcast_fusion.5), kind=kLoop, calls=%fused_computation.2.clone.1 | loop fusion | flops 14082048 | bytes 327680 | tf_op jit(solution)/shard_map/while/body/eval_jaxpr/reduce_sum | solution.py:18
  44.2 18.8 %all-to-all-done = bf16[128,4,3584]{2,1,0:T(4,128)(2,1)} async-done(((bf16[128,4,3584]{2,1,0:T(4,128)(2,1)}), bf16[128,4,3584]{2,1,0:T(4,128)(2,1)}, u32[]{:S(2)}, u32[]{:S(2)}) %all-to-all-start) | async-done | bytes 3670048 | tf_op jit(solution)/shard_map/all_to_all | solution.py:27
  62.9 6.7 %reshape.27 = bf16[512,3584]{1,0:T(8,128)(2,1)} reshape(bf16[128,4,3584]{2,1,0:T(4,128)(2,1)} %all-to-all-done) | data formatting | bytes 7340032 | tf_op jit(solution)/shard_map/reshape | solution.py:26
  69.6 10.9 %fusion.5 = (f32[512]{0:T(512)S(1)}, f32[512,1152]{1,0:T(8,128)}) fusion(bf16[512,3584]{1,0:T(8,128)(2,1)} %reshape.27, bf16[1152,3584]{1,0:T(8,128)(2,1)} %param.7), kind=kOutput, calls=%fused_computation.19 | convolution fusion | flops 4228447744 | bytes 14288896 | tf_op jit(solution)/shard_map/dot_general | solution.py:32
  80.5 62.5 %pmax.7 = f32[512]{0:T(512)S(1)} all-reduce(f32[512]{0:T(512)S(1)} %get-tuple-element.56), channel_id=1, replica_groups=mesh['tok'=16,'voc'=8] {'tok','voc'}, use_global_device_ids=true, to_apply=%region_8.9 | all-reduce | flops 512 | bytes 4096 | tf_op jit(solution)/shard_map/pmax | solution.py:42
  143.0 2.3 fusion.2
  145.3 62.7 %psum.15 = f32[512]{0:T(512)S(1)} all-reduce(f32[512]{0:T(512)S(1)} %get-tuple-element.42), channel_id=1, replica_groups=mesh['tok'=16,'voc'=8] {'tok','voc'}, use_global_device_ids=true, to_apply=%region_10.11 | all-reduce | flops 512 | bytes 4096 | tf_op jit(solution)/shard_map/psum | solution.py:43
  208.0 2.6 fusion.4
  210.5 10.4 %fusion.6 = f32[512,3584]{1,0:T(8,128)} fusion(bf16[512,1152]{1,0:T(8,128)(2,1)S(1)} %fusion.4, bf16[1152,3584]{1,0:T(8,128)(2,1)} %param.7), kind=kOutput, calls=%fused_computation.20 | convolution fusion | flops 4227858432 | bytes 16777216 | tf_op jit(solution)/shard_map/dot_general | solution.py:58
  221.0 6.7 %convolution_convert_fusion = bf16[1152,3584]{1,0:T(8,128)(2,1)} fusion(bf16[512,1152]{1,0:T(8,128)(2,1)S(1)} %fusion.4, bf16[512,3584]{1,0:T(8,128)(2,1)S(1)} %copy-done), kind=kOutput, calls=%fused_computation.6 | convolution fusion | flops 4231987200 | bytes 13107200 | tf_op jit(solution)/shard_map/dot_general | solution.py:54
  227.7 110.2 %all-reduce.3 = (f32[512]{0:T(512)S(1)}, bf16[512,3584]{1,0:T(8,128)(2,1)}) all-reduce(f32[512]{0:T(512)S(1)} %get-tuple-element.41, f32[512,3584]{1,0:T(8,128)} %fusion.6), channel_id=1, replica_groups=mesh['tok'=16,'voc'=8] {'tok','voc'}, use_global_device_ids=true, to_apply=%region_5.6 | all-reduce | flops 1835520 | bytes 11014144 | tf_op jit(solution)/shard_map/psum | solution.py:43
  337.8 0.6 dynamic_slice.11
  338.4 1.4 dynamic-slice_convert_fusion
  (36 shorter events, 0.6 us)
Async XLA Ops:
  4.2 11.6 %copy-start.1 = (s32[512,64]{0,1:T(8,128)S(1)}, s32[512,64]{0,1:T(8,128)}, u32[]{:S(2)}) copy-start(s32[512,64]{0,1:T(8,128)} %param.8) | copy-start | bytes 393220
  4.2 11.8 %copy-start.2 = (f32[512,64]{0,1:T(8,128)S(1)}, f32[512,64]{0,1:T(8,128)}, u32[]{:S(2)}) copy-start(f32[512,64]{0,1:T(8,128)} %param.9) | copy-start | bytes 393220
  4.2 58.7 %all-to-all-start = ((bf16[128,4,3584]{2,1,0:T(4,128)(2,1)}), bf16[128,4,3584]{2,1,0:T(4,128)(2,1)}, u32[]{:S(2)}, u32[]{:S(2)}) async-start(bf16[128,4,3584]{2,1,0:T(4,128)(2,1)} %stack.2), calls=%async_computation | async-start | bytes 7340032 | tf_op jit(solution)/shard_map/all_to_all | solution.py:27
  210.5 10.4 %copy-start = (bf16[512,3584]{1,0:T(8,128)(2,1)S(1)}, bf16[512,3584]{1,0:T(8,128)(2,1)}, u32[]{:S(2)}) copy-start(bf16[512,3584]{1,0:T(8,128)(2,1)} %reshape.27) | copy-start | bytes 11010052
